TPU v7x, 32 devices: a whole 2x2x4 slice. The times are simulated.
32 devices in a mesh: ens: 2 (over x), tile: 8 (over z, y), comp: 2 (over core).
Axes of the slice: x: 2, y: 2, z: 4, core: 2. Of those that a mesh axis runs over, the one named last changes fastest.
Arguments:
- increment: bfloat16 [64, 128, 256], P(('ens', 'tile'), None, 'comp'), parts along dimension 0, may hold values from -6 to 6
- land_sea: int32 [32, 128], P('tile'), may hold values 0 or 1
- kernel_x: float32 [41, 256], P(None, 'comp'), may hold values from -1 to 1
- kernel_y: float32 [41, 256], P(None, 'comp'), may hold values from -1 to 1
- balance: bfloat16 [8, 256, 256], P('tile', 'comp'), may hold values from -0.375 to 0.375
Outputs:
- filtered: bfloat16 [64, 128, 256], P('ens', 'tile', 'comp'), parts along dimension 0
There are 2 independent parts, one for each index of `ens`. A program takes and returns all parts, laid end to end along the dimension named above; an argument that names none is the same for every part. Nothing has to cross between parts.
All inputs are finite; a program needn't handle non-finite values. No bound on the sum of `land_sea` on one device may be relied on, other than what follows from the above.
Results may differ from a plain program's by a relative error of at most 0.0057.
Values may be sent and summed in bfloat16 or wider, within the bound.
No kernel may reach another device: no remote copies, remote signals or barrier semaphores. Data moves between devices by JAX's collectives and lax.ppermute only.
A program may use at most 64 MiB of HBM per device.

v0:
```python
import jax
import jax.numpy as jnp
from jax import lax
from jax.sharding import PartitionSpec as P


def zonal_filter(values, kernel):
    taps = kernel.shape[0]
    half_taps = (taps - 1) // 2
    total = jnp.zeros(values.shape, jnp.float32)
    for offset in range(taps):
        total = total + kernel[offset] * jnp.roll(values, half_taps - offset, axis=1)
    return total


def meridional_filter(values, kernel):
    taps = kernel.shape[0]
    half_taps = (taps - 1) // 2
    rows_all = values.shape[0]
    padded = jnp.pad(values, ((half_taps, half_taps), (0, 0), (0, 0)))
    total = jnp.zeros(values.shape, jnp.float32)
    for offset in range(taps):
        total = total + kernel[offset] * padded[offset : offset + rows_all]
    return total


def to_columns(row_bands):
    return lax.all_to_all(row_bands, "tile", split_axis=1, concat_axis=0, tiled=True)


def per_device(increment, land_sea, kernel_x, kernel_y, balance):
    sea = land_sea.astype(jnp.bfloat16)[:, :, None]
    masked = increment * sea
    zonal = (zonal_filter(masked, kernel_x) * sea.astype(jnp.float32)).astype(jnp.bfloat16)
    own_block = balance[0]
    mixed_rows = jnp.dot(
        lax.all_gather(zonal, "comp", axis=2, tiled=True),
        own_block.T,
        preferred_element_type=jnp.float32,
    )
    mixed = to_columns(mixed_rows.astype(jnp.bfloat16))
    return meridional_filter(mixed, kernel_y).astype(jnp.bfloat16)


def solution(mesh):
    return jax.shard_map(
        per_device,
        mesh=mesh,
        in_specs=(
            P(("ens", "tile"), None, "comp"),
            P("tile", None),
            P(None, "comp"),
            P(None, "comp"),
            P("tile", "comp", None),
        ),
        out_specs=P("ens", "tile", "comp"),
        check_vma=False,
    )
```

profile of v0, /device:TPU:0, one launch (start us, length us, event | category | flops | bytes accessed | tf_op | source)
XLA Modules:
  0.0 26.5 jit_solution(1189334224262708944)
XLA Ops:
  0.0 0.0 copy-start
  0.0 0.7 %fusion.1 = (f32[4,128]{1,0:T(4,128)S(1)}, bf16[4,128]{1,0:T(4,128)(2,1)S(1)}) fusion(s32[4,128]{1,0:T(4,128)} %param.6), kind=kLoop, calls=%fused_computation.127 | loop fusion | flops 1024 | bytes 5120 | tf_op jit(solution)/shard_map/convert_element_type | solution.py:34
  0.7 1.0 %broadcast_multiply_fusion = bf16[4,128,128]{2,1,0:T(8,128)(2,1)S(1)} fusion(bf16[4,128,128]{2,1,0:T(8,128)(2,1)} %param.5, bf16[4,128]{1,0:T(4,128)(2,1)S(1)} %get-tuple-element.6), kind=kLoop, calls=%fused_computation.44 | loop fusion | flops 65536 | bytes 263168 | tf_op jit(solution)/shard_map/mul | solution.py:33
  3.0 0.0 copy-start.2
  3.1 0.7 %copy-done.2 = f32[41,128]{1,0:T(8,128)S(1)} copy-done((f32[41,128]{1,0:T(8,128)S(1)}, f32[41,128]{1,0:T(8,128)}, u32[]{:S(2)}) %copy-start.2) | copy-done | bytes 21016
  3.8 0.0 copy-start.1
  3.8 0.9 %copy-done.1 = bf16[4,128,128]{2,1,0:T(8,128)(2,1)S(1)} copy-done((bf16[4,128,128]{2,1,0:T(8,128)(2,1)S(1)}, bf16[4,128,128]{2,1,0:T(8,128)(2,1)}, u32[]{:S(2)}) %copy-start.1) | copy-done | bytes 131096
  4.7 2.4 %multiply_convert_fusion = bf16[4,128,128]{2,1,0:T(8,128)(2,1)S(1)} fusion(bf16[4,108,128]{2,1,0:T(8,128)(2,1)S(1)} %get-tuple-element.8, bf16[4,20,128]{2,1,0:T(8,128)(2,1)S(1)} %get-tuple-element.10, bf16[4,109,128]{2,1,0:T(8,128)(2,1)S(1)} %get-tuple-element.12, bf16[4,19,128]{2,1,0:T(8,128)(2,1)S(1)} %get-tuple-element.14, ...), kind=kLoop, calls=%fused_computation.42 | loop fusion | flops 16187392 | bytes 5529088 | tf_op jit(solution)/shard_map/convert_element_type | solution.py:34
  7.1 2.1 %all_gather.3 = bf16[4,128,256]{2,1,0:T(8,128)(2,1)S(1)} all-gather(bf16[4,128,128]{2,1,0:T(8,128)(2,1)S(1)} %multiply_convert_fusion), channel_id=1, replica_groups=mesh['ens'=2,'tile'=8,'comp'=2] {'comp'}, dimensions={2}, use_global_device_ids=true | all-gather | bytes 393216 | tf_op jit(solution)/shard_map/all_gather | solution.py:37
  9.2 0.0 copy-done
  9.2 0.2 convolution_convert_fusion
  9.4 0.8 %copy.7 = bf16[4,128,128]{2,0,1:T(4,128)(2,1)} copy(bf16[4,128,128]{2,1,0:T(8,128)(2,1)S(1)} %convolution_convert_fusion) | data formatting | bytes 262144 | tf_op jit(solution)/shard_map/convert_element_type | solution.py:41
  10.2 0.0 copy-start.3
  10.2 7.3 %all-to-all-start = ((bf16[4,128,128]{2,0,1:T(4,128)(2,1)}), bf16[4,128,128]{2,0,1:T(4,128)(2,1)S(1)}, u32[]{:S(2)}, u32[]{:S(2)}) async-start(bf16[4,128,128]{2,0,1:T(4,128)(2,1)} %copy.7), calls=%async_computation | async-start | bytes 262144 | tf_op jit(solution)/shard_map/all_to_all | solution.py:28
  17.5 0.0 copy-done.3
  17.6 7.3 %all-to-all-done = bf16[4,128,128]{2,0,1:T(4,128)(2,1)S(1)} async-done(((bf16[4,128,128]{2,0,1:T(4,128)(2,1)}), bf16[4,128,128]{2,0,1:T(4,128)(2,1)S(1)}, u32[]{:S(2)}, u32[]{:S(2)}) %all-to-all-start) | async-done | bytes 131104 | tf_op jit(solution)/shard_map/all_to_all | solution.py:28
  24.9 1.6 %add_convert_fusion = bf16[32,16,128]{2,1,0:T(8,128)(2,1)} fusion(bf16[32,16,128]{2,1,0:T(8,128)(2,1)S(1)} %bitcast.174, f32[128]{0:T(128)S(1)} %get-tuple-element.126, f32[128]{0:T(128)S(1)} %get-tuple-element.127, f32[128]{0:T(128)S(1)} %get-tuple-element.88, f32[128]{0:T(128)S(1)} %get-tuple-element.89, f32[128]{0:T(128)S(1)} %get-tuple-element.90, ...), kind=kLoop, calls=%fused_computation.41 | loop fusion | flops 8060928 | bytes 283136 | tf_op jit(solution)/shard_map/convert_element_type | solution.py:42
  (47 shorter events, 1.1 us)
Async XLA Ops:
  0.0 9.2 %copy-start = (bf16[1,128,256]{2,1,0:T(8,128)(2,1)S(1)}, bf16[1,128,256]{2,1,0:T(8,128)(2,1)}, u32[]{:S(2)}) copy-start(bf16[1,128,256]{2,1,0:T(8,128)(2,1)} %param.9) | copy-start | bytes 196612
  3.0 0.7 %copy-start.2 = (f32[41,128]{1,0:T(8,128)S(1)}, f32[41,128]{1,0:T(8,128)}, u32[]{:S(2)}) copy-start(f32[41,128]{1,0:T(8,128)} %param.7) | copy-start | bytes 62980
  3.8 0.9 %copy-start.1 = (bf16[4,128,128]{2,1,0:T(8,128)(2,1)S(1)}, bf16[4,128,128]{2,1,0:T(8,128)(2,1)}, u32[]{:S(2)}) copy-start(bf16[4,128,128]{2,1,0:T(8,128)(2,1)} %param.5) | copy-start | bytes 393220
  10.2 7.3 %copy-start.3 = (f32[41,128]{1,0:T(8,128)S(1)}, f32[41,128]{1,0:T(8,128)}, u32[]{:S(2)}) copy-start(f32[41,128]{1,0:T(8,128)} %param.8) | copy-start | bytes 62980
  10.2 14.7 %all-to-all-start = ((bf16[4,128,128]{2,0,1:T(4,128)(2,1)}), bf16[4,128,128]{2,0,1:T(4,128)(2,1)S(1)}, u32[]{:S(2)}, u32[]{:S(2)}) async-start(bf16[4,128,128]{2,0,1:T(4,128)(2,1)} %copy.7), calls=%async_computation | async-start | bytes 262144 | tf_op jit(solution)/shard_map/all_to_all | solution.py:28
where the time goes:
time: 26.9 us; the launch traced here: 26.5 us
  starting transfers between devices  7.32 us (27%)
  waiting for transfers between devices  7.28 us (27%)
  other arithmetic  5.79 us (22%)
  local copies, waits for them, and re-layouts  3.41 us (13%)
  blocking collectives  2.09 us (8%)
  between operations  0.41 us (2%)
    all_to_all x1, starting transfers between devices, to_columns(): lax.all_to_all(row_bands, 'tile', split_axis=1, concat_axis=0, tiled=True)  7.32 us
    all_to_all x1, waiting for transfers between devices, to_columns(): lax.all_to_all(row_bands, 'tile', split_axis=1, concat_axis=0, tiled=True)  7.28 us
    convert_element_type x1, other arithmetic, per_device(): (zonal_filter(masked, kernel_x) * sea.astype(jnp.float32)).astype(jnp.bfl...  2.42 us
    all_gather x1, blocking collectives, per_device(): lax.all_gather(zonal, 'comp', axis=2, tiled=True)  2.09 us
    convert_element_type x1, other arithmetic, per_device(): return meridional_filter(mixed, kernel_y).astype(jnp.bfloat16)  1.63 us
    unnamed x8, local copies, waits for them, and re-layouts  1.54 us
    mul x1, other arithmetic, per_device(): masked = increment * sea  1.03 us
    slice x40, local copies, waits for them, and re-layouts, zonal_filter(): jnp.roll(values, half_taps - offset, axis=1)  1.03 us
  transfers between devices with their start and end apart: 1, of which 1 were waited for; matrix products, arithmetic and copies ran while one was open for 0% of the time, Pallas kernels for 0%

commit v1 on v0

--- a/solution.py
+++ b/solution.py
@@ -25,7 +25,15 @@
 
 
 def to_columns(row_bands):
-    return lax.all_to_all(row_bands, "tile", split_axis=1, concat_axis=0, tiled=True)
+    return jnp.concatenate(
+        lax.all_to_all(
+            jnp.stack(jnp.split(row_bands, lax.axis_size("tile"), axis=1)),
+            axis_name="tile",
+            split_axis=0,
+            concat_axis=0,
+        ),
+        axis=0,
+    )
 
 
 def per_device(increment, land_sea, kernel_x, kernel_y, balance):

time: 26.9 us -> 30.9 us (1.15)
  local copies, waits for them, and re-layouts: 3.41 us -> 7.49 us
    unnamed x8 -> x15, local copies, waits for them, and re-layouts: 1.54 us -> 5.8 us
    convert_element_type x1 -> x0, local copies, waits for them, and re-layouts: 0.76 us -> none  [per_device(): mixed = to_columns(mixed_rows.astype(jnp.bfloat16))]
    another operation x0 -> x1, local copies, waits for them, and re-layouts: none -> 0.61 us  [to_columns(): jnp.stack(jnp.split(row_bands, lax.axis_size('tile'), axis=1))]
where the time goes in v1:
time: 30.9 us; the launch traced here: 30.5 us
  local copies, waits for them, and re-layouts  7.49 us (24%)
  starting transfers between devices  7.32 us (24%)
  waiting for transfers between devices  7.28 us (24%)
  other arithmetic  5.71 us (18%)
  blocking collectives  2.09 us (7%)
  between operations  0.41 us (1%)
    all_to_all x1, starting transfers between devices, to_columns(): lax.all_to_all(jnp.stack(jnp.split(row_bands, lax.axis_size('tile'), axis...  7.32 us
    all_to_all x1, waiting for transfers between devices, to_columns(): lax.all_to_all(jnp.stack(jnp.split(row_bands, lax.axis_size('tile'), axis...  7.28 us
    unnamed x15, local copies, waits for them, and re-layouts  5.8 us
    convert_element_type x1, other arithmetic, per_device(): (zonal_filter(masked, kernel_x) * sea.astype(jnp.float32)).astype(jnp.bfl...  2.42 us
    all_gather x1, blocking collectives, per_device(): lax.all_gather(zonal, 'comp', axis=2, tiled=True)  2.09 us
    convert_element_type x1, other arithmetic, per_device(): return meridional_filter(mixed, kernel_y).astype(jnp.bfloat16)  1.54 us
    mul x1, other arithmetic, per_device(): masked = increment * sea  1.03 us
    slice x40, local copies, waits for them, and re-layouts, zonal_filter(): jnp.roll(values, half_taps - offset, axis=1)  1.03 us
  transfers between devices with their start and end apart: 1, of which 1 were waited for; matrix products, arithmetic and copies ran while one was open for 0% of the time, Pallas kernels for 0%

profile of v1, /device:TPU:0, one launch (start us, length us, event | category | flops | bytes accessed | tf_op | source)
XLA Modules:
  0.0 30.5 jit_solution(12755372123217632514)
XLA Ops:
  0.0 0.0 copy-start
  0.0 0.7 %fusion.1 = (f32[4,128]{1,0:T(4,128)S(1)}, bf16[4,128]{1,0:T(4,128)(2,1)S(1)}) fusion(s32[4,128]{1,0:T(4,128)} %param.6), kind=kLoop, calls=%fused_computation.143 | loop fusion | flops 1024 | bytes 5120 | tf_op jit(solution)/shard_map/convert_element_type | solution.py:42
  0.7 1.0 %broadcast_multiply_fusion = bf16[4,128,128]{2,1,0:T(8,128)(2,1)S(1)} fusion(bf16[4,128,128]{2,1,0:T(8,128)(2,1)} %param.5, bf16[4,128]{1,0:T(4,128)(2,1)S(1)} %get-tuple-element.6), kind=kLoop, calls=%fused_computation.44 | loop fusion | flops 65536 | bytes 263168 | tf_op jit(solution)/shard_map/mul | solution.py:41
  3.0 0.0 copy-start.2
  3.1 0.7 %copy-done.2 = f32[41,128]{1,0:T(8,128)S(1)} copy-done((f32[41,128]{1,0:T(8,128)S(1)}, f32[41,128]{1,0:T(8,128)}, u32[]{:S(2)}) %copy-start.2) | copy-done | bytes 21016
  3.8 0.0 copy-start.1
  3.8 0.9 %copy-done.1 = bf16[4,128,128]{2,1,0:T(8,128)(2,1)S(1)} copy-done((bf16[4,128,128]{2,1,0:T(8,128)(2,1)S(1)}, bf16[4,128,128]{2,1,0:T(8,128)(2,1)}, u32[]{:S(2)}) %copy-start.1) | copy-done | bytes 131096
  4.7 2.4 %multiply_convert_fusion = bf16[4,128,128]{2,1,0:T(8,128)(2,1)S(1)} fusion(bf16[4,108,128]{2,1,0:T(8,128)(2,1)S(1)} %get-tuple-element.8, bf16[4,20,128]{2,1,0:T(8,128)(2,1)S(1)} %get-tuple-element.10, bf16[4,109,128]{2,1,0:T(8,128)(2,1)S(1)} %get-tuple-element.12, bf16[4,19,128]{2,1,0:T(8,128)(2,1)S(1)} %get-tuple-element.14, ...), kind=kLoop, calls=%fused_computation.42 | loop fusion | flops 16187392 | bytes 5529088 | tf_op jit(solution)/shard_map/convert_element_type | solution.py:42
  7.1 2.1 %all_gather.3 = bf16[4,128,256]{2,1,0:T(8,128)(2,1)S(1)} all-gather(bf16[4,128,128]{2,1,0:T(8,128)(2,1)S(1)} %multiply_convert_fusion), channel_id=1, replica_groups=mesh['ens'=2,'tile'=8,'comp'=2] {'comp'}, dimensions={2}, use_global_device_ids=true | all-gather | bytes 393216 | tf_op jit(solution)/shard_map/all_gather | solution.py:45
  9.2 0.0 copy-done
  9.2 0.2 convolution_convert_fusion
  9.4 0.6 %constant_dynamic-update-slice_fusion.7 = bf16[8,4,16,128]{3,2,1,0:T(8,128)(2,1)} fusion(bf16[4,128,128]{2,1,0:T(8,128)(2,1)S(1)} %convolution_convert_fusion), kind=kLoop, calls=%fused_computation.52 | loop fusion | bytes 32768
  10.0 0.6 %constant_dynamic-update-slice_fusion.6 = bf16[8,4,16,128]{3,2,1,0:T(8,128)(2,1)} fusion(bf16[8,4,16,128]{3,2,1,0:T(8,128)(2,1)} %constant_dynamic-update-slice_fusion.7, bf16[4,128,128]{2,1,0:T(8,128)(2,1)S(1)} %convolution_convert_fusion), kind=kLoop, calls=%fused_computation.51 | loop fusion | bytes 32768
  10.7 0.6 %constant_dynamic-update-slice_fusion.5 = bf16[8,4,16,128]{3,2,1,0:T(8,128)(2,1)} fusion(bf16[8,4,16,128]{3,2,1,0:T(8,128)(2,1)} %constant_dynamic-update-slice_fusion.6, bf16[4,128,128]{2,1,0:T(8,128)(2,1)S(1)} %convolution_convert_fusion), kind=kLoop, calls=%fused_computation.50 | loop fusion | bytes 32768
  11.3 0.6 %constant_dynamic-update-slice_fusion.4 = bf16[8,4,16,128]{3,2,1,0:T(8,128)(2,1)} fusion(bf16[8,4,16,128]{3,2,1,0:T(8,128)(2,1)} %constant_dynamic-update-slice_fusion.5, bf16[4,128,128]{2,1,0:T(8,128)(2,1)S(1)} %convolution_convert_fusion), kind=kLoop, calls=%fused_computation.49 | loop fusion | bytes 32768
  11.9 0.6 %constant_dynamic-update-slice_fusion.3 = bf16[8,4,16,128]{3,2,1,0:T(8,128)(2,1)} fusion(bf16[8,4,16,128]{3,2,1,0:T(8,128)(2,1)} %constant_dynamic-update-slice_fusion.4, bf16[4,128,128]{2,1,0:T(8,128)(2,1)S(1)} %convolution_convert_fusion), kind=kLoop, calls=%fused_computation.48 | loop fusion | bytes 32768
  12.5 0.6 %constant_dynamic-update-slice_fusion.2 = bf16[8,4,16,128]{3,2,1,0:T(8,128)(2,1)} fusion(bf16[8,4,16,128]{3,2,1,0:T(8,128)(2,1)} %constant_dynamic-update-slice_fusion.3, bf16[4,128,128]{2,1,0:T(8,128)(2,1)S(1)} %convolution_convert_fusion), kind=kLoop, calls=%fused_computation.47 | loop fusion | bytes 32768
  13.1 0.6 %constant_dynamic-update-slice_fusion.1 = bf16[8,4,16,128]{3,2,1,0:T(8,128)(2,1)} fusion(bf16[8,4,16,128]{3,2,1,0:T(8,128)(2,1)} %constant_dynamic-update-slice_fusion.2, bf16[4,128,128]{2,1,0:T(8,128)(2,1)S(1)} %convolution_convert_fusion), kind=kLoop, calls=%fused_computation.46 | loop fusion | bytes 32768
  13.7 0.6 %constant_dynamic-update-slice_fusion = bf16[8,4,16,128]{3,2,1,0:T(8,128)(2,1)} fusion(bf16[8,4,16,128]{3,2,1,0:T(8,128)(2,1)} %constant_dynamic-update-slice_fusion.1, bf16[4,128,128]{2,1,0:T(8,128)(2,1)S(1)} %convolution_convert_fusion), kind=kLoop, calls=%fused_computation.45 | loop fusion | bytes 32768 | tf_op jit(solution)/shard_map/stack | solution.py:30
  14.3 0.0 copy-start.3
  14.3 7.3 %all-to-all-start = ((bf16[8,4,16,128]{3,2,1,0:T(8,128)(2,1)}), bf16[8,4,16,128]{3,2,1,0:T(8,128)(2,1)S(1)}, u32[]{:S(2)}, u32[]{:S(2)}) async-start(bf16[8,4,16,128]{3,2,1,0:T(8,128)(2,1)} %constant_dynamic-update-slice_fusion), calls=%async_computation | async-start | bytes 262144 | tf_op jit(solution)/shard_map/all_to_all | solution.py:29
  21.6 0.0 copy-done.3
  21.7 7.3 %all-to-all-done = bf16[8,4,16,128]{3,2,1,0:T(8,128)(2,1)S(1)} async-done(((bf16[8,4,16,128]{3,2,1,0:T(8,128)(2,1)}), bf16[8,4,16,128]{3,2,1,0:T(8,128)(2,1)S(1)}, u32[]{:S(2)}, u32[]{:S(2)}) %all-to-all-start) | async-done | bytes 131104 | tf_op jit(solution)/shard_map/all_to_all | solution.py:29
  29.0 1.5 %add_convert_fusion = bf16[32,16,128]{2,1,0:T(8,128)(2,1)} fusion(bf16[32,16,128]{2,1,0:T(8,128)(2,1)S(1)} %bitcast.202, f32[128]{0:T(128)S(1)} %get-tuple-element.126, f32[128]{0:T(128)S(1)} %get-tuple-element.127, f32[128]{0:T(128)S(1)} %get-tuple-element.88, f32[128]{0:T(128)S(1)} %get-tuple-element.89, f32[128]{0:T(128)S(1)} %get-tuple-element.90, ...), kind=kLoop, calls=%fused_computation.41 | loop fusion | flops 8060928 | bytes 283136 | tf_op jit(solution)/shard_map/convert_element_type | solution.py:50
  (46 shorter events, 1.1 us)
Async XLA Ops:
  0.0 9.2 %copy-start = (bf16[1,128,256]{2,1,0:T(8,128)(2,1)S(1)}, bf16[1,128,256]{2,1,0:T(8,128)(2,1)}, u32[]{:S(2)}) copy-start(bf16[1,128,256]{2,1,0:T(8,128)(2,1)} %param.9) | copy-start | bytes 196612
  3.0 0.7 %copy-start.2 = (f32[41,128]{1,0:T(8,128)S(1)}, f32[41,128]{1,0:T(8,128)}, u32[]{:S(2)}) copy-start(f32[41,128]{1,0:T(8,128)} %param.7) | copy-start | bytes 62980
  3.8 0.9 %copy-start.1 = (bf16[4,128,128]{2,1,0:T(8,128)(2,1)S(1)}, bf16[4,128,128]{2,1,0:T(8,128)(2,1)}, u32[]{:S(2)}) copy-start(bf16[4,128,128]{2,1,0:T(8,128)(2,1)} %param.5) | copy-start | bytes 393220
  14.3 7.3 %copy-start.3 = (f32[41,128]{1,0:T(8,128)S(1)}, f32[41,128]{1,0:T(8,128)}, u32[]{:S(2)}) copy-start(f32[41,128]{1,0:T(8,128)} %param.8) | copy-start | bytes 62980
  14.3 14.7 %all-to-all-start = ((bf16[8,4,16,128]{3,2,1,0:T(8,128)(2,1)}), bf16[8,4,16,128]{3,2,1,0:T(8,128)(2,1)S(1)}, u32[]{:S(2)}, u32[]{:S(2)}) async-start(bf16[8,4,16,128]{3,2,1,0:T(8,128)(2,1)} %constant_dynamic-update-slice_fusion), calls=%async_computation | async-start | bytes 262144 | tf_op jit(solution)/shard_map/all_to_all | solution.py:29
